TPU v7x, 512 devices: a whole 4x8x8 slice. The times are simulated.
512 devices in a mesh: table: 64 (over y, z), expert: 8 (over x, core).
Axes of the slice: x: 4, y: 8, z: 8, core: 2. Of those that a mesh axis runs over, the one named last changes fastest.
Arguments:
- table: bfloat16 [64, 512, 256], P('table'), may hold values from -127 to 127, as said below
- row_scale: float32 [64, 512], P('table'), may hold values from 0.3 to 3
- windows: int32 [64, 8, 256], P('table', 'expert'), may hold values from 0 to 511, as said below
- bag_idx: int32 [64, 8, 8192, 8], P('table', 'expert'), may hold values from 0 to 255
- bag_len: int32 [64, 8, 8192], P('table', 'expert'), may hold values from 1 to 8
- feat_gain: float32 [64, 256], replicated, may hold values from 0.03 to 0.3
- norm_gain: float32 [256], replicated, may hold values from 0.5 to 1.5
- expert_ids: int32 [8, 8192, 1], P('expert', 'table'), may hold values from 0 to 63; in each aligned block of 128 rows (0 to 127, 128 to 255, ..., all dimensions but the last counted through in order) at most 4 rows name the same one
- w_in: bfloat16 [64, 256, 4096], P('table', None, 'expert'), may hold values from -0.375 to 0.375
- w_out: bfloat16 [64, 4096, 256], P('table', 'expert'), may hold values from -0.09375 to 0.09375
- w_tow1: bfloat16 [3, 256, 256], replicated, may hold values from -0.375 to 0.375
- w_tow2: float32 [3, 256], replicated, may hold values from -1.5 to 1.5
- targets: float32 [8, 8192, 3], P('expert', 'table'), may hold values from 0 to 1
Outputs:
- predictions: float32 [8, 8192, 3], P('expert', 'table')
- grad_table: float32 [64, 512, 256], P('table', 'expert')
- grad_w_in: float32 [64, 256, 4096], P('table', None, 'expert')
- grad_w_out: float32 [64, 4096, 256], P('table', 'expert')
Inputs may be any that keep to these rules, and one draw needn't show every extreme that they name: `table`: every entry is an integer. Each row windows[f, g] holds 256 distinct row numbers of feature f's table. `expert_ids`: in each aligned block of 128 samples (the samples of one device) no expert is named by more than 4 samples.
All inputs are finite; a program needn't handle non-finite values.
Results may differ from a plain program's by a relative error of at most 0.02.
Values may be sent and summed in bfloat16 or wider, within the bound.
No kernel may reach another device: no remote copies, remote signals or barrier semaphores. Data moves between devices by JAX's collectives and lax.ppermute only.
A program may use at most 128 MiB of HBM per device.

v0:
```python
import math
import jax
import jax.numpy as jnp
from jax import lax
from jax.sharding import PartitionSpec as P

code_range = 127.0


def silu_slope(values):
    sigma = jax.nn.sigmoid(values)
    return sigma * (1.0 + values * (1.0 - sigma))


def bag_counts(indices, lengths, window):
    total = indices.shape[0]
    block = math.gcd(total, 512)
    positions = jnp.arange(window, dtype=jnp.int32)
    slots = jnp.arange(indices.shape[1], dtype=jnp.int32)

    def count_block(operands):
        block_idx, block_len = operands
        live = (slots[None, :] < block_len[:, None]).astype(jnp.float32)
        hits = (block_idx[:, :, None] == positions[None, None, :]).astype(jnp.float32)
        return jnp.sum(hits * live[:, :, None], axis=1).astype(jnp.bfloat16)

    blocked = lax.map(
        count_block,
        (
            indices.reshape(total // block, block, indices.shape[1]),
            lengths.reshape(total // block, block),
        ),
    )
    return blocked.reshape(total, window)


def dispatch(buffer):
    arrived = lax.all_to_all(buffer, "table", split_axis=0, concat_axis=0, tiled=True)
    columns = lax.all_gather(arrived[None], "expert", axis=0, tiled=True)
    return columns.reshape(-1, buffer.shape[-1])


def column_sum(term_fn, local_rows):
    return lax.psum_scatter(
        term_fn(jnp.int32(0), lax.axis_size("expert") * local_rows).astype(jnp.bfloat16),
        "expert",
        scatter_dimension=0,
        tiled=True,
    ).astype(jnp.float32)


def send_back(result, experts, capacity):
    rows_back = result.astype(jnp.bfloat16).reshape(experts, capacity, result.shape[-1])
    arrived = lax.all_to_all(rows_back, "table", split_axis=0, concat_axis=0, tiled=True)
    return arrived.reshape(experts * capacity, result.shape[-1])


def local(
    table,
    row_scale,
    windows,
    bag_idx,
    bag_len,
    feat_gain,
    norm_gain,
    expert_ids,
    w_in,
    w_out,
    w_tow1,
    w_tow2,
    targets,
):
    owners = lax.axis_size("table")
    samples = expert_ids.shape[1]
    capacity = max(2, 2 * samples // owners)
    local_rows = owners * capacity
    contract_rows = (((0,), (0,)), ((), ()))
    contract_cols = (((1,), (1,)), ((), ()))
    window = windows[0, 0]
    picked = jnp.take(table[0], window, axis=0).astype(jnp.float32)
    scales = jnp.take(row_scale[0], window)
    dequant = (picked * scales[:, None] / code_range).astype(jnp.bfloat16)
    counts = bag_counts(bag_idx[0, 0], bag_len[0, 0], window.shape[0])
    pooled = jnp.dot(counts, dequant, preferred_element_type=jnp.float32).astype(jnp.bfloat16)
    features = lax.all_to_all(
        pooled.reshape(owners, samples, pooled.shape[-1]),
        "table",
        split_axis=0,
        concat_axis=0,
        tiled=True,
    )
    summed = jnp.sum(features.astype(jnp.float32) * feat_gain[:, None, :], axis=0)
    inverse = lax.rsqrt(jnp.mean(summed * summed, axis=-1, keepdims=True) + 1e-05)
    normed = (summed * inverse * norm_gain).astype(jnp.bfloat16)
    chosen = expert_ids[0, :, 0]
    member = (chosen[:, None] == jnp.arange(owners, dtype=jnp.int32)[None, :]).astype(jnp.int32)
    ranks = jnp.cumsum(member, axis=0) - member
    slot_of = jnp.sum(ranks * member, axis=1)
    target_slot = chosen * capacity + slot_of
    placing = (jnp.arange(local_rows, dtype=jnp.int32)[:, None] == target_slot[None, :]).astype(
        jnp.bfloat16
    )
    outgoing = jnp.dot(placing, normed, preferred_element_type=jnp.float32).astype(jnp.bfloat16)
    gathered = dispatch(outgoing.reshape(owners, capacity, outgoing.shape[-1]))
    weight_in = w_in[0]
    weight_out = w_out[0]
    pre_act = jnp.dot(gathered, weight_in, preferred_element_type=jnp.float32)
    hidden = jax.nn.silu(pre_act).astype(jnp.bfloat16)

    def forward_term(start, count):
        return jnp.dot(hidden, weight_out, preferred_element_type=jnp.float32)

    expert_out = send_back(column_sum(forward_term, local_rows), owners, capacity)
    mixture = lax.dot_general(
        placing, expert_out, contract_rows, preferred_element_type=jnp.float32
    )
    joined = (normed.astype(jnp.float32) + mixture).astype(jnp.bfloat16)
    tower_pre = jnp.einsum("be,kem->kbm", joined, w_tow1, preferred_element_type=jnp.float32)
    logits = jnp.sum(jax.nn.silu(tower_pre) * w_tow2[:, None, :], axis=-1)
    predicted = jnp.stack(
        [jax.nn.sigmoid(logits[0]), jax.nn.sigmoid(logits[1]), logits[2]], axis=-1
    )
    logit_grad = predicted - targets[0]
    tower_grad = (logit_grad.T[:, :, None] * w_tow2[:, None, :] * silu_slope(tower_pre)).astype(
        jnp.bfloat16
    )
    joined_grad = jnp.einsum(
        "kbm,kem->be", tower_grad, w_tow1, preferred_element_type=jnp.float32
    ).astype(jnp.bfloat16)
    back_rows = jnp.dot(placing, joined_grad, preferred_element_type=jnp.float32).astype(
        jnp.bfloat16
    )
    gathered_grad = dispatch(back_rows.reshape(owners, capacity, back_rows.shape[-1]))
    grad_hidden = lax.dot_general(
        gathered_grad, weight_out, contract_cols, preferred_element_type=jnp.float32
    )
    grad_pre = (grad_hidden * silu_slope(pre_act)).astype(jnp.bfloat16)
    grad_out = lax.dot_general(
        hidden, gathered_grad, contract_rows, preferred_element_type=jnp.float32
    )
    grad_in = lax.dot_general(gathered, grad_pre, contract_rows, preferred_element_type=jnp.float32)

    def backward_term(start, count):
        return lax.dot_general(
            grad_pre, weight_in, contract_cols, preferred_element_type=jnp.float32
        )

    input_grad = send_back(column_sum(backward_term, local_rows), owners, capacity)
    mixture_grad = lax.dot_general(
        placing, input_grad, contract_rows, preferred_element_type=jnp.float32
    )
    normed_grad = joined_grad.astype(jnp.float32) + mixture_grad
    scaled_grad = normed_grad * norm_gain
    summed_grad = inverse * (
        scaled_grad
        - summed * inverse * inverse * jnp.mean(scaled_grad * summed, axis=-1, keepdims=True)
    )
    feature_grad = (summed_grad[None, :, :] * feat_gain[:, None, :]).astype(jnp.bfloat16)
    returned = lax.all_to_all(
        feature_grad, "table", split_axis=0, concat_axis=0, tiled=True
    ).reshape(owners * samples, feature_grad.shape[-1])
    window_grad = lax.dot_general(
        counts, returned, contract_rows, preferred_element_type=jnp.float32
    )
    row_select = (jnp.arange(table.shape[1], dtype=jnp.int32)[:, None] == window[None, :]).astype(
        jnp.float32
    )
    row_grad = jnp.dot(row_select, window_grad, precision=lax.Precision.HIGHEST)
    table_grad = lax.psum_scatter(
        row_grad.astype(jnp.bfloat16), "expert", scatter_dimension=0, tiled=True
    ).astype(jnp.float32)
    return (predicted[None], table_grad[None], grad_in[None], grad_out[None])


def solution(mesh):
    in_specs = (
        P("table", None, None),
        P("table", None),
        P("table", "expert", None),
        P("table", "expert", None, None),
        P("table", "expert", None),
        P(),
        P(),
        P("expert", "table", None),
        P("table", None, "expert"),
        P("table", "expert", None),
        P(),
        P(),
        P("expert", "table", None),
    )
    out_specs = (
        P("expert", "table", None),
        P("table", "expert", None),
        P("table", None, "expert"),
        P("table", "expert", None),
    )
    return jax.shard_map(local, mesh=mesh, in_specs=in_specs, out_specs=out_specs, check_vma=False)
```

profile of v0, /device:TPU:8, one launch (start us, length us, event | category | flops | bytes accessed | tf_op | source)
XLA Modules:
  0.0 661.4 jit_solution(6694098426931538434)
XLA Ops:
  10.0 75.1 %while.11 = (s32[]{:T(128)}, bf16[16,512,256]{2,1,0:T(8,128)(2,1)}, s32[16,512,8]{1,2,0:T(8,128)}, s32[16,512]{1,0:T(8,128)S(1)}, s32[]{:T(128)}) while((s32[]{:T(128)}, bf16[16,512,256]{2,1,0:T(8,128)(2,1)}, s32[16,512,8]{1,2,0:T(8,128)}, s32[16,512]{1,0:T(8,128)S(1)}, s32[]{:T(128)}) %tuple.50), condition=%wide.region_2.3_spmd.clone, body=%wide.region_0.0_spmd.clone.sunk | while | flops 3022850 | bytes 940613 | solution.py:27
  34.5 3.0 select_reduce_fusion.3
  39.2 3.0 select_reduce_fusion.3
  88.2 5.5 convolution_convert_fusion
  93.7 16.9 %all-to-all-start = ((bf16[64,128,256]{2,1,0:T(8,128)(2,1)}), bf16[64,128,256]{2,1,0:T(8,128)(2,1)}, u32[]{:S(2)}, u32[]{:S(2)}) async-start(bf16[64,128,256]{2,1,0:T(8,128)(2,1)} %bitcast.88), calls=%async_computation | async-start | bytes 8388608 | tf_op jit(solution)/shard_map/all_to_all | solution.py:85
  111.2 126.4 %all-to-all-done = bf16[64,128,256]{2,1,0:T(8,128)(2,1)} async-done(((bf16[64,128,256]{2,1,0:T(8,128)(2,1)}), bf16[64,128,256]{2,1,0:T(8,128)(2,1)}, u32[]{:S(2)}, u32[]{:S(2)}) %all-to-all-start) | async-done | bytes 4194336 | tf_op jit(solution)/shard_map/all_to_all | solution.py:85
  237.6 3.1 multiply_reduce_fusion
  241.1 27.0 %all_to_all.30 = bf16[64,4,256]{2,1,0:T(4,128)(2,1)} all-to-all(bf16[64,4,256]{2,1,0:T(4,128)(2,1)S(1)} %reshape.210), channel_id=1, replica_groups=mesh['table'=64,'expert'=8] {'table'}, dimensions={0} | all-to-all | bytes 262144 | tf_op jit(solution)/shard_map/all_to_all | solution.py:38
  268.2 20.6 %all-gather.5.cloned.1.call-done = bf16[512,4,256]{2,1,0:T(4,128)(2,1)} async-done(((bf16[64,4,256]{2,1,0:T(4,128)(2,1)}), bf16[512,4,256]{2,1,0:T(4,128)(2,1)}) %all-gather.5.cloned.1.call-update) | async-done | bytes 1048592 | tf_op jit(solution)/shard_map/all_gather | solution.py:39
  290.2 3.1 multiply_convert_fusion.2
  296.4 37.5 %reduce-scatter.4.cloned.1.call-done = bf16[256,256]{1,0:T(8,128)(2,1)} async-done(((bf16[2048,256]{1,0:T(8,128)(2,1)}), bf16[256,256]{1,0:T(8,128)(2,1)}) %reduce-scatter.4.cloned.1.call-update) | async-done | bytes 131088 | tf_op jit(solution)/shard_map/reduce_scatter | solution.py:44
  334.9 24.9 %all_to_all.31 = bf16[64,4,256]{2,1,0:T(4,128)(2,1)S(1)} all-to-all(bf16[64,4,256]{2,1,0:T(4,128)(2,1)S(1)} %reshape.212), channel_id=1, replica_groups=mesh['table'=64,'expert'=8] {'table'}, dimensions={0} | all-to-all | bytes 262144 | tf_op jit(solution)/shard_map/all_to_all | solution.py:54
  361.0 17.1 %all_to_all.32 = bf16[64,4,256]{2,1,0:T(4,128)(2,1)} all-to-all(bf16[64,4,256]{2,1,0:T(4,128)(2,1)S(1)} %reshape.214), channel_id=1, replica_groups=mesh['table'=64,'expert'=8] {'table'}, dimensions={0} | all-to-all | bytes 262144 | tf_op jit(solution)/shard_map/all_to_all | solution.py:38
  378.3 18.9 %all-gather.7.cloned.1.call-done = bf16[512,4,256]{2,1,0:T(4,128)(2,1)} async-done(((bf16[64,4,256]{2,1,0:T(4,128)(2,1)}), bf16[512,4,256]{2,1,0:T(4,128)(2,1)}) %all-gather.7.cloned.1.call-update) | async-done | bytes 1048592 | tf_op jit(solution)/shard_map/all_gather | solution.py:39
  398.6 5.2 multiply_convert_fusion.1
  403.8 3.3 convolution_convert_fusion.1
  407.2 37.6 %reduce-scatter.6.cloned.1.call-done = bf16[256,256]{1,0:T(8,128)(2,1)} async-done(((bf16[2048,256]{1,0:T(8,128)(2,1)}), bf16[256,256]{1,0:T(8,128)(2,1)}) %reduce-scatter.6.cloned.1.call-update) | async-done | bytes 131088 | tf_op jit(solution)/shard_map/reduce_scatter | solution.py:44
  445.7 25.0 %all_to_all.33 = bf16[64,4,256]{2,1,0:T(4,128)(2,1)S(1)} all-to-all(bf16[64,4,256]{2,1,0:T(4,128)(2,1)S(1)} %reshape.216), channel_id=1, replica_groups=mesh['table'=64,'expert'=8] {'table'}, dimensions={0} | all-to-all | bytes 262144 | tf_op jit(solution)/shard_map/all_to_all | solution.py:54
  471.2 3.4 multiply_convert_fusion
  474.6 6.4 all-to-all-start.5
  481.7 105.1 %all-to-all-done.5 = bf16[64,128,256]{2,1,0:T(8,128)(2,1)} async-done(((bf16[64,128,256]{2,1,0:T(8,128)(2,1)}), bf16[64,128,256]{2,1,0:T(8,128)(2,1)}, u32[]{:S(2)}, u32[]{:S(2)}) %all-to-all-start.5) | async-done | bytes 4194336 | tf_op jit(solution)/shard_map/all_to_all | solution.py:159
  586.8 4.7 fusion.35
  592.7 3.4 convolution_bitcast_fusion.1
  597.6 55.8 %reduce-scatter.8.cloned.1.call-done = bf16[64,256]{1,0:T(8,128)(2,1)} async-done(((bf16[512,256]{1,0:T(8,128)(2,1)}), bf16[64,256]{1,0:T(8,128)(2,1)}) %reduce-scatter.8.cloned.1.call-update) | async-done | bytes 32784 | tf_op jit(solution)/shard_map/reduce_scatter | solution.py:169
  (185 shorter events, 89.7 us)
Async XLA Ops:
  7.2 352.7 %copy-start = (bf16[3,256,256]{2,1,0:T(8,128)(2,1)S(1)}, bf16[3,256,256]{2,1,0:T(8,128)(2,1)}, u32[]{:S(2)}) copy-start(bf16[3,256,256]{2,1,0:T(8,128)(2,1)} %param.25) | copy-start | bytes 1179652
  9.9 75.1 %copy-start.1 = (f32[1,512]{1,0:T(1,128)S(1)}, f32[1,512]{1,0:T(1,128)}, u32[]{:S(2)}) copy-start(f32[1,512]{1,0:T(1,128)} %param.16) | copy-start | bytes 6148
  9.9 77.1 %copy-start.2 = (bf16[1,512,256]{2,1,0:T(8,128)(2,1)S(1)}, bf16[1,512,256]{2,1,0:T(8,128)(2,1)}, u32[]{:S(2)}) copy-start(bf16[1,512,256]{2,1,0:T(8,128)(2,1)} %param.15) | copy-start | bytes 786436
  10.0 78.2 %copy-start.8 = (s32[1,1,256]{2,1,0:T(1,128)S(1)}, s32[1,1,256]{2,1,0:T(1,128)}, u32[]{:S(2)}) copy-start(s32[1,1,256]{2,1,0:T(1,128)} %param.17) | copy-start | bytes 3076
  93.7 17.0 %copy-start.10 = (s32[1,128,1]{1,2,0:T(1,128)S(1)}, s32[1,128,1]{1,2,0:T(1,128)}, u32[]{:S(2)}) copy-start(s32[1,128,1]{1,2,0:T(1,128)} %param.22) | copy-start | bytes 1540
  93.7 143.9 %copy-start.6 = (f32[64,256]{1,0:T(8,128)S(1)}, f32[64,256]{1,0:T(8,128)}, u32[]{:S(2)}) copy-start(f32[64,256]{1,0:T(8,128)} %param.20) | copy-start | bytes 196612
  93.7 143.9 %all-to-all-start = ((bf16[64,128,256]{2,1,0:T(8,128)(2,1)}), bf16[64,128,256]{2,1,0:T(8,128)(2,1)}, u32[]{:S(2)}, u32[]{:S(2)}) async-start(bf16[64,128,256]{2,1,0:T(8,128)(2,1)} %bitcast.88), calls=%async_computation | async-start | bytes 8388608 | tf_op jit(solution)/shard_map/all_to_all | solution.py:85
  110.6 130.2 %copy-start.9 = (f32[256]{0:T(256)S(1)}, f32[256]{0:T(256)}, u32[]{:S(2)}) copy-start(f32[256]{0:T(256)} %param.21) | copy-start | bytes 3076
  110.6 179.5 %copy-start.7 = (bf16[1,256,512]{2,1,0:T(8,128)(2,1)S(1)}, bf16[1,256,512]{2,1,0:T(8,128)(2,1)}, u32[]{:S(2)}) copy-start(bf16[1,256,512]{2,1,0:T(8,128)(2,1)} %param.23) | copy-start | bytes 786436
  110.7 178.2 %all-gather.5.cloned.1.call-start = ((), (), s32[]{:S(2)}) async-start(), calls=%async_computation.12 | async-start | bytes 1179648 | tf_op jit(solution)/shard_map/all_gather | solution.py:39
  268.1 65.9 %reduce-scatter.4.cloned.1.call-start = ((), (), s32[]{:S(2)}) async-start(), calls=%async_computation.9 | async-start | bytes 1179648 | tf_op jit(solution)/shard_map/reduce_scatter | solution.py:44
  290.2 3.2 copy-start.5
  290.2 4.5 copy-start.12
  293.3 1.3 copy-start.3
  293.3 66.5 %copy-start.13 = (f32[3,256]{1,0:T(4,128)S(1)}, f32[3,256]{1,0:T(4,128)}, u32[]{:S(2)}) copy-start(f32[3,256]{1,0:T(4,128)} %param.26) | copy-start | bytes 9220
  294.7 65.8 %copy-start.11 = (f32[1,128,3]{1,0,2:T(1,128)S(1)}, f32[1,128,3]{1,0,2:T(1,128)}, u32[]{:S(2)}) copy-start(f32[1,128,3]{1,0,2:T(1,128)} %param.27) | copy-start | bytes 4612
  296.4 100.9 %all-gather.7.cloned.1.call-start = ((), (), s32[]{:S(2)}) async-start(), calls=%async_computation.13 | async-start | bytes 1179648 | tf_op jit(solution)/shard_map/all_gather | solution.py:39
  378.1 66.6 %reduce-scatter.6.cloned.1.call-start = ((), (), s32[]{:S(2)}) async-start(), calls=%async_computation.10 | async-start | bytes 1179648 | tf_op jit(solution)/shard_map/reduce_scatter | solution.py:44
  474.6 112.1 %all-to-all-start.5 = ((bf16[64,128,256]{2,1,0:T(8,128)(2,1)}), bf16[64,128,256]{2,1,0:T(8,128)(2,1)}, u32[]{:S(2)}, u32[]{:S(2)}) async-start(bf16[64,128,256]{2,1,0:T(8,128)(2,1)} %multiply_convert_fusion), calls=%async_computation.7 | async-start | bytes 8388608 | tf_op jit(solution)/shard_map/all_to_all | solution.py:159
  481.0 172.4 %reduce-scatter.8.cloned.1.call-start = ((), (), s32[]{:S(2)}) async-start(), calls=%async_computation.11 | async-start | bytes 294912 | tf_op jit(solution)/shard_map/reduce_scatter | solution.py:169
  591.5 4.6 copy-start.4
Sparse Core Ops, SparseCore 0:
  268.2 20.5 all-gather.4
  296.5 37.4 reduce-scatter.3
  378.2 18.9 all-gather.6
  407.3 37.4 reduce-scatter.5
  592.8 60.6 reduce-scatter.7
where the time goes:
time: 663 us; the launch traced here: 661 us
  waiting for transfers between devices  402 us (61%)
  blocking collectives  94 us (14%)
  other arithmetic  58.2 us (9%)
  local copies, waits for them, and re-layouts  37.5 us (6%)
  matrix products  31.3 us (5%)
  starting transfers between devices  23.7 us (4%)
  between operations  14.1 us (2%)
    all_to_all x1, waiting for transfers between devices, local(): lax.all_to_all(pooled.reshape(owners, samples, pooled.shape[-1]), 'table'...  126 us
    all_to_all x1, waiting for transfers between devices, local(): lax.all_to_all(feature_grad, 'table', split_axis=0, concat_axis=0, tiled=...  105 us
    reduce_scatter x2, waiting for transfers between devices, column_sum(): lax.psum_scatter(term_fn(jnp.int32(0), lax.axis_size('expert') * local_ro...  75.1 us
    reduce_scatter x1, waiting for transfers between devices, local(): lax.psum_scatter(row_grad.astype(jnp.bfloat16), 'expert', scatter_dimensi...  55.8 us
    all_to_all x2, blocking collectives, send_back(): lax.all_to_all(rows_back, 'table', split_axis=0, concat_axis=0, tiled=True)  49.9 us
    reduce_sum x16, other arithmetic, count_block(): return jnp.sum(hits * live[:, :, None], axis=1).astype(jnp.bfloat16)  47.3 us
    all_to_all x2, blocking collectives, dispatch(): lax.all_to_all(buffer, 'table', split_axis=0, concat_axis=0, tiled=True)  44 us
    all_gather x2, waiting for transfers between devices, dispatch(): columns = lax.all_gather(arrived[None], 'expert', axis=0, tiled=True)  39.6 us
  transfers between devices with their start and end apart: 7, of which 7 were waited for; matrix products, arithmetic and copies ran while one was open for 1% of the time, Pallas kernels for 0%

commit v1 on v0

--- a/solution.py
+++ b/solution.py
@@ -5,6 +5,24 @@
 from jax.sharding import PartitionSpec as P
 
 code_range = 127.0
+
+
+def ring_gather(value, axis, dim):
+    ways, here, step = (lax.axis_size(axis), lax.axis_index(axis), value.shape[dim])
+    shape = [n * ways if d == dim else n for d, n in enumerate(value.shape)]
+    full = lax.dynamic_update_slice_in_dim(
+        jnp.zeros(shape, value.dtype), value, here * step, axis=dim
+    )
+    going_up = going_down = value
+    for far in range(1, ways // 2 + 1):
+        going_up = lax.ppermute(going_up, axis, [(d, (d + 1) % ways) for d in range(ways)])
+        full = lax.dynamic_update_slice_in_dim(full, going_up, (here - far) % ways * step, axis=dim)
+        if 2 * far < ways:
+            going_down = lax.ppermute(going_down, axis, [(d, (d - 1) % ways) for d in range(ways)])
+            full = lax.dynamic_update_slice_in_dim(
+                full, going_down, (here + far) % ways * step, axis=dim
+            )
+    return full
 
 
 def silu_slope(values):
@@ -36,7 +54,7 @@
 
 def dispatch(buffer):
     arrived = lax.all_to_all(buffer, "table", split_axis=0, concat_axis=0, tiled=True)
-    columns = lax.all_gather(arrived[None], "expert", axis=0, tiled=True)
+    columns = ring_gather(arrived[None], "expert", 0)
     return columns.reshape(-1, buffer.shape[-1])
 
 

time: 663 us -> 644 us (0.971)
  starting transfers between devices: 23.7 us -> 68.4 us
  waiting for transfers between devices: 402 us -> 365 us
  blocking collectives: 94 us -> 66.5 us
    all_gather x2 -> x0, waiting for transfers between devices: 39.6 us -> none  [dispatch(): columns = lax.all_gather(arrived[None], 'expert', axis=0, tiled=True)]
    all_to_all x2 -> x1, blocking collectives: 44 us -> 16.8 us  [dispatch(): lax.all_to_all(buffer, 'table', split_axis=0, concat_axis=0, tiled=True)]
    all_to_all x0 -> x1, starting transfers between devices: none -> 27.2 us  [dispatch(): lax.all_to_all(buffer, 'table', split_axis=0, concat_axis=0, tiled=True)]
    ppermute x0 -> x14, waiting for transfers between devices: none -> 25.5 us  [the longest x8 25.5 us: ring_gather(): lax.ppermute(going_up, axis, [(d, (d + 1) % ways) for d in range(ways)])]
    reduce_scatter x2, waiting for transfers between devices: 75.1 us -> 55 us  [column_sum(): lax.psum_scatter(term_fn(jnp.int32(0), lax.axis_size('expert') * local_ro...]
    ppermute x0 -> x14, starting transfers between devices: none -> 17.8 us  [the longest x6 17.7 us: ring_gather(): lax.ppermute(going_down, axis, [(d, (d - 1) % ways) for d in range(ways)])]
    all_to_all x0 -> x1, waiting for transfers between devices: none -> 11.7 us  [dispatch(): lax.all_to_all(buffer, 'table', split_axis=0, concat_axis=0, tiled=True)]
    reduce_scatter x1, waiting for transfers between devices: 55.8 us -> 44.8 us  [local(): lax.psum_scatter(row_grad.astype(jnp.bfloat16), 'expert', scatter_dimensi...]
  transfers between devices with their start and end apart: 7 -> 20, of which waited for: 7 -> 14; matrix products, arithmetic and copies ran while one was open for 1% -> 1% of each run, Pallas kernels for 0% -> 0%
where the time goes in v1:
time: 644 us; the launch traced here: 642 us
  waiting for transfers between devices  365 us (57%)
  starting transfers between devices  68.4 us (11%)
  blocking collectives  66.5 us (10%)
  other arithmetic  58.2 us (9%)
  local copies, waits for them, and re-layouts  37.8 us (6%)
  matrix products  31.3 us (5%)
  between operations  14.3 us (2%)
    all_to_all x1, waiting for transfers between devices, local(): lax.all_to_all(pooled.reshape(owners, samples, pooled.shape[-1]), 'table'...  118 us
    all_to_all x1, waiting for transfers between devices, local(): lax.all_to_all(feature_grad, 'table', split_axis=0, concat_axis=0, tiled=...  110 us
    reduce_scatter x2, waiting for transfers between devices, column_sum(): lax.psum_scatter(term_fn(jnp.int32(0), lax.axis_size('expert') * local_ro...  55 us
    all_to_all x2, blocking collectives, send_back(): lax.all_to_all(rows_back, 'table', split_axis=0, concat_axis=0, tiled=True)  49.8 us
    reduce_sum x16, other arithmetic, count_block(): return jnp.sum(hits * live[:, :, None], axis=1).astype(jnp.bfloat16)  47.3 us
    reduce_scatter x1, waiting for transfers between devices, local(): lax.psum_scatter(row_grad.astype(jnp.bfloat16), 'expert', scatter_dimensi...  44.8 us
    all_to_all x1, starting transfers between devices, dispatch(): lax.all_to_all(buffer, 'table', split_axis=0, concat_axis=0, tiled=True)  27.2 us
    ppermute x8, waiting for transfers between devices, ring_gather(): lax.ppermute(going_up, axis, [(d, (d + 1) % ways) for d in range(ways)])  25.5 us
  transfers between devices with their start and end apart: 20, of which 14 were waited for; matrix products, arithmetic and copies ran while one was open for 1% of the time, Pallas kernels for 0%

profile of v1, /device:TPU:8, one launch (start us, length us, event | category | flops | bytes accessed | tf_op | source)
XLA Modules:
  0.0 642.0 jit_solution(2391561098147133246)
XLA Ops:
  10.0 75.2 %while.11 = (s32[]{:T(128)}, bf16[16,512,256]{2,1,0:T(8,128)(2,1)}, s32[16,512,8]{1,2,0:T(8,128)}, s32[16,512]{1,0:T(8,128)S(1)}, s32[]{:T(128)}) while((s32[]{:T(128)}, bf16[16,512,256]{2,1,0:T(8,128)(2,1)}, s32[16,512,8]{1,2,0:T(8,128)}, s32[16,512]{1,0:T(8,128)S(1)}, s32[]{:T(128)}) %tuple.45), condition=%wide.region_2.3_spmd.clone, body=%wide.region_0.0_spmd.clone.sunk | while | flops 3022850 | bytes 940613 | solution.py:45
  88.3 5.5 convolution_convert_fusion
  93.8 16.9 %all-to-all-start = ((bf16[64,128,256]{2,1,0:T(8,128)(2,1)}), bf16[64,128,256]{2,1,0:T(8,128)(2,1)}, u32[]{:S(2)}, u32[]{:S(2)}) async-start(bf16[64,128,256]{2,1,0:T(8,128)(2,1)} %bitcast.92), calls=%async_computation | async-start | bytes 8388608 | tf_op jit(solution)/shard_map/all_to_all | solution.py:103
  111.2 118.3 %all-to-all-done = bf16[64,128,256]{2,1,0:T(8,128)(2,1)} async-done(((bf16[64,128,256]{2,1,0:T(8,128)(2,1)}), bf16[64,128,256]{2,1,0:T(8,128)(2,1)}, u32[]{:S(2)}, u32[]{:S(2)}) %all-to-all-start) | async-done | bytes 4194336 | tf_op jit(solution)/shard_map/all_to_all | solution.py:103
  229.5 3.1 multiply_reduce_fusion
  233.7 27.2 %all-to-all-start.1 = ((bf16[64,4,256]{2,1,0:T(4,128)(2,1)}), bf16[64,4,256]{2,1,0:T(4,128)(2,1)S(1)}, u32[]{:S(2)}, u32[]{:S(2)}) async-start(bf16[64,4,256]{2,1,0:T(4,128)(2,1)} %reshape.210), calls=%async_computation.1 | async-start | bytes 262144 | tf_op jit(solution)/shard_map/all_to_all | solution.py:56
  261.1 11.7 %all-to-all-done.1 = bf16[64,4,256]{2,1,0:T(4,128)(2,1)S(1)} async-done(((bf16[64,4,256]{2,1,0:T(4,128)(2,1)}), bf16[64,4,256]{2,1,0:T(4,128)(2,1)S(1)}, u32[]{:S(2)}, u32[]{:S(2)}) %all-to-all-start.1) | async-done | bytes 131104 | tf_op jit(solution)/shard_map/all_to_all | solution.py:56
  289.7 5.5 collective-permute-done.6
  295.5 3.2 multiply_convert_fusion.2
  301.8 27.5 %reduce-scatter.4.cloned.1.call-done = bf16[256,256]{1,0:T(8,128)(2,1)} async-done(((bf16[2048,256]{1,0:T(8,128)(2,1)}), bf16[256,256]{1,0:T(8,128)(2,1)}) %reduce-scatter.4.cloned.1.call-update) | async-done | bytes 131088 | tf_op jit(solution)/shard_map/reduce_scatter | solution.py:62
  330.2 24.9 %all_to_all.30 = bf16[64,4,256]{2,1,0:T(4,128)(2,1)S(1)} all-to-all(bf16[64,4,256]{2,1,0:T(4,128)(2,1)S(1)} %reshape.212), channel_id=1, replica_groups=mesh['table'=64,'expert'=8] {'table'}, dimensions={0} | all-to-all | bytes 262144 | tf_op jit(solution)/shard_map/all_to_all | solution.py:72
  356.3 16.8 %all_to_all.31 = bf16[64,4,256]{2,1,0:T(4,128)(2,1)S(1)} all-to-all(bf16[64,4,256]{2,1,0:T(4,128)(2,1)S(1)} %reshape.214), channel_id=1, replica_groups=mesh['table'=64,'expert'=8] {'table'}, dimensions={0} | all-to-all | bytes 262144 | tf_op jit(solution)/shard_map/all_to_all | solution.py:56
  378.8 3.0 collective-permute-start.10
  390.1 5.4 collective-permute-done.13
  395.9 5.2 multiply_convert_fusion.1
  401.1 3.3 convolution_convert_fusion.1
  404.4 27.5 %reduce-scatter.6.cloned.1.call-done = bf16[256,256]{1,0:T(8,128)(2,1)} async-done(((bf16[2048,256]{1,0:T(8,128)(2,1)}), bf16[256,256]{1,0:T(8,128)(2,1)}) %reduce-scatter.6.cloned.1.call-update) | async-done | bytes 131088 | tf_op jit(solution)/shard_map/reduce_scatter | solution.py:62
  432.9 24.8 %all_to_all.32 = bf16[64,4,256]{2,1,0:T(4,128)(2,1)S(1)} all-to-all(bf16[64,4,256]{2,1,0:T(4,128)(2,1)S(1)} %reshape.216), channel_id=1, replica_groups=mesh['table'=64,'expert'=8] {'table'}, dimensions={0} | all-to-all | bytes 262144 | tf_op jit(solution)/shard_map/all_to_all | solution.py:72
  458.2 3.4 multiply_convert_fusion
  461.6 6.4 %all-to-all-start.5 = ((bf16[64,128,256]{2,1,0:T(8,128)(2,1)}), bf16[64,128,256]{2,1,0:T(8,128)(2,1)}, u32[]{:S(2)}, u32[]{:S(2)}) async-start(bf16[64,128,256]{2,1,0:T(8,128)(2,1)} %multiply_convert_fusion), calls=%async_computation.7 | async-start | bytes 8388608 | tf_op jit(solution)/shard_map/all_to_all | solution.py:177
  468.7 109.8 %all-to-all-done.5 = bf16[64,128,256]{2,1,0:T(8,128)(2,1)} async-done(((bf16[64,128,256]{2,1,0:T(8,128)(2,1)}), bf16[64,128,256]{2,1,0:T(8,128)(2,1)}, u32[]{:S(2)}, u32[]{:S(2)}) %all-to-all-start.5) | async-done | bytes 4194336 | tf_op jit(solution)/shard_map/all_to_all | solution.py:177
  578.5 4.7 fusion.35
  584.4 3.4 convolution_bitcast_fusion.1
  589.3 44.8 %reduce-scatter.8.cloned.1.call-done = bf16[64,256]{1,0:T(8,128)(2,1)} async-done(((bf16[512,256]{1,0:T(8,128)(2,1)}), bf16[64,256]{1,0:T(8,128)(2,1)}) %reduce-scatter.8.cloned.1.call-update) | async-done | bytes 32784 | tf_op jit(solution)/shard_map/reduce_scatter | solution.py:187
  (226 shorter events, 125.0 us)
Async XLA Ops:
  7.2 348.0 %copy-start = (bf16[3,256,256]{2,1,0:T(8,128)(2,1)S(1)}, bf16[3,256,256]{2,1,0:T(8,128)(2,1)}, u32[]{:S(2)}) copy-start(bf16[3,256,256]{2,1,0:T(8,128)(2,1)} %param.25) | copy-start | bytes 1179652
  10.0 78.3 %copy-start.8 = (s32[1,1,256]{2,1,0:T(1,128)S(1)}, s32[1,1,256]{2,1,0:T(1,128)}, u32[]{:S(2)}) copy-start(s32[1,1,256]{2,1,0:T(1,128)} %param.17) | copy-start | bytes 3076
  93.8 135.7 %copy-start.6 = (f32[64,256]{1,0:T(8,128)S(1)}, f32[64,256]{1,0:T(8,128)}, u32[]{:S(2)}) copy-start(f32[64,256]{1,0:T(8,128)} %param.20) | copy-start | bytes 196612
  93.8 135.7 %all-to-all-start = ((bf16[64,128,256]{2,1,0:T(8,128)(2,1)}), bf16[64,128,256]{2,1,0:T(8,128)(2,1)}, u32[]{:S(2)}, u32[]{:S(2)}) async-start(bf16[64,128,256]{2,1,0:T(8,128)(2,1)} %bitcast.92), calls=%async_computation | async-start | bytes 8388608 | tf_op jit(solution)/shard_map/all_to_all | solution.py:103
  110.8 122.0 %copy-start.9 = (f32[256]{0:T(256)S(1)}, f32[256]{0:T(256)}, u32[]{:S(2)}) copy-start(f32[256]{0:T(256)} %param.21) | copy-start | bytes 3076
  233.7 39.0 %all-to-all-start.1 = ((bf16[64,4,256]{2,1,0:T(4,128)(2,1)}), bf16[64,4,256]{2,1,0:T(4,128)(2,1)S(1)}, u32[]{:S(2)}, u32[]{:S(2)}) async-start(bf16[64,4,256]{2,1,0:T(4,128)(2,1)} %reshape.210), calls=%async_computation.1 | async-start | bytes 262144 | tf_op jit(solution)/shard_map/all_to_all | solution.py:56
  260.9 68.4 %reduce-scatter.4.cloned.1.call-start = ((), (), s32[]{:S(2)}) async-start(), calls=%async_computation.9 | async-start | bytes 1179648 | tf_op jit(solution)/shard_map/reduce_scatter | solution.py:62
  272.7 5.6 collective-permute-start
  272.7 5.6 collective-permute-start.1
  278.3 5.6 collective-permute-start.2
  278.3 5.6 collective-permute-start.3
  283.9 5.6 collective-permute-start.4
  283.9 5.7 collective-permute-start.5
  289.5 5.6 collective-permute-start.6
  301.8 130.2 %reduce-scatter.6.cloned.1.call-start = ((), (), s32[]{:S(2)}) async-start(), calls=%async_computation.10 | async-start | bytes 1179648 | tf_op jit(solution)/shard_map/reduce_scatter | solution.py:62
  373.1 5.6 collective-permute-start.7
  373.1 5.7 collective-permute-start.8
  378.7 5.6 collective-permute-start.9
  378.8 5.6 collective-permute-start.10
  384.3 5.6 collective-permute-start.11
  384.4 5.6 collective-permute-start.12
  389.9 5.6 collective-permute-start.13
  461.6 116.8 %all-to-all-start.5 = ((bf16[64,128,256]{2,1,0:T(8,128)(2,1)}), bf16[64,128,256]{2,1,0:T(8,128)(2,1)}, u32[]{:S(2)}, u32[]{:S(2)}) async-start(bf16[64,128,256]{2,1,0:T(8,128)(2,1)} %multiply_convert_fusion), calls=%async_computation.7 | async-start | bytes 8388608 | tf_op jit(solution)/shard_map/all_to_all | solution.py:177
  468.1 166.0 %reduce-scatter.8.cloned.1.call-start = ((), (), s32[]{:S(2)}) async-start(), calls=%async_computation.11 | async-start | bytes 294912 | tf_op jit(solution)/shard_map/reduce_scatter | solution.py:187
  (10 other events, 358.1 us)
Sparse Core Ops, SparseCore 0:
  301.9 27.3 reduce-scatter.3
  404.6 27.3 reduce-scatter.5
  584.5 49.5 reduce-scatter.7
